TPU v7x, 256 devices: a whole 4x4x8 slice. The times are simulated.
256 devices in a mesh: sec: 16 (over x, y), vel: 16 (over z, core).
Axes of the slice: x: 4, y: 4, z: 8, core: 2. Of those that a mesh axis runs over, the one named last changes fastest.
Arguments:
- distribution: float32 [13824, 4096], P('vel', 'sec'), may hold values from -6 to 6
- collision: float32 [4096], P('sec'), may hold values from 0.05 to 2
- lower_blocks: float32 [25, 4096], P(None, 'sec'), may hold values from -0.6 to 0.6
- upper_blocks: float32 [25, 4096], P(None, 'sec'), may hold values from -0.6 to 0.6
- diag_inverse: float32 [25, 4096], P(None, 'sec'), may hold values from -0.2 to 1.4
Outputs:
- new_distribution: float32 [13824, 4096], P('vel', 'sec')
- macro: float32 [5, 4096], P(None, 'sec')
All inputs are finite; a program needn't handle non-finite values.
Results may differ from a plain program's by a relative error of at most 0.0003.
Values sent between devices are 32-bit elements; how exact they have to be, the bound alone decides.
No kernel may reach another device: no remote copies, remote signals or barrier semaphores. Data moves between devices by JAX's collectives and lax.ppermute only.
A program may use at most 64 MiB of HBM per device.

v0:
```python
import math
import jax
import jax.numpy as jnp
import numpy as np
from jax import lax
from jax.sharding import PartitionSpec as P

NXI = 24
TUBES = 128
JACOBI = 4
NEWTON = 2
HIGH = lax.Precision.HIGHEST
pseudo_rate = 1.0


def passed_along(block, axis, distance):
    devices = range(lax.axis_size(axis))
    route = [(i - distance, i) for i in devices if i - distance in devices]
    return lax.ppermute(block, axis, route)


def extended(array, sides, width):
    for axis, dim in sides:
        count, length = (lax.axis_size(axis), array.shape[dim])
        up = [(i, (i + 1) % count) for i in range(count - 1)]
        down = [(j, i) for i, j in up]
        last = lax.slice_in_dim(array, length - width, length, axis=dim)
        first = lax.slice_in_dim(array, 0, width, axis=dim)
        before = lax.ppermute(last, axis, up)
        after = lax.ppermute(first, axis, down)
        array = jnp.concatenate([before, array, after], axis=dim)
    return array


def hermite_rule(count):
    quarter = math.pi ** (-0.25)
    found = []
    last_slope = 1.0
    for index in range(count // 2):
        if index == 0:
            guess = math.sqrt(2.0 * count + 1.0) - 1.85575 * (2.0 * count + 1.0) ** (-0.16667)
        elif index == 1:
            guess = guess - 1.14 * count**0.426 / guess
        elif index == 2:
            guess = 1.86 * guess - 0.86 * found[0][0]
        elif index == 3:
            guess = 1.91 * guess - 0.91 * found[1][0]
        else:
            guess = 2.0 * guess - found[index - 2][0]
        for repeat in range(60):
            current = quarter
            previous = 0.0
            for order in range(count):
                older = previous
                previous = current
                current = (
                    guess * math.sqrt(2.0 / (order + 1)) * previous
                    - math.sqrt(order / (order + 1.0)) * older
                )
            last_slope = math.sqrt(2.0 * count) * previous
            guess = guess - current / last_slope
        found.append((guess, 2.0 / (last_slope * last_slope)))
    positive = found[::-1]
    points = [-pair[0] for pair in found] + [pair[0] for pair in positive]
    weights = [pair[1] for pair in found] + [pair[1] for pair in positive]
    return (np.array(points), np.array(weights))


def node_tables(axis_points):
    points, weights = hermite_rule(axis_points)
    node_index = np.arange(axis_points**3)
    idx_x = node_index % axis_points
    idx_z = node_index // axis_points % axis_points
    idx_y = node_index // (axis_points * axis_points)
    along_x = points[idx_x]
    along_y = points[idx_y]
    along_z = points[idx_z]
    node_weight = weights[idx_x] * weights[idx_y] * weights[idx_z] / math.pi**1.5
    energy = along_x**2 + along_y**2 + along_z**2 - 1.5
    moment_basis = np.stack([along_x * 0.0 + 1.0, along_x, along_y, along_z, energy])
    norm_scale = np.array([1.0, 0.5, 0.5, 0.5, 1.5])
    return (
        along_x,
        node_weight,
        moment_basis * node_weight[None, :],
        moment_basis / norm_scale[:, None],
    )


def apply_block(matrices, vector):
    shaped = matrices.reshape((5, 5) + vector.shape[1:])
    return jnp.sum(shaped * vector[None], axis=1)


def affine_combine(earlier_map, later_map):
    return (later_map[0] * earlier_map[0], later_map[0] * earlier_map[1] + later_map[1])


def newton_sums(loaded, signed, shift_mass, shift_flow):
    growth = jnp.exp(shift_mass + shift_flow * signed)
    scaled = loaded * growth
    excess = loaded * (growth - 1.0)
    return jnp.stack(
        [
            jnp.sum(scaled),
            jnp.sum(scaled * signed),
            jnp.sum(scaled * signed * signed),
            jnp.sum(excess),
            jnp.sum(excess * signed),
        ]
    )


def newton_update(shift_mass, shift_flow, sums, goal_mass, goal_flow):
    resid_mass = sums[3] - goal_mass
    resid_flow = sums[4] - goal_flow
    determinant = sums[0] * sums[2] - sums[1] * sums[1]
    new_mass = shift_mass - (sums[2] * resid_mass - sums[1] * resid_flow) / determinant
    new_flow = shift_flow - (sums[0] * resid_flow - sums[1] * resid_mass) / determinant
    return (new_mass, new_flow)


def received(block, distance):
    count = lax.axis_size("sec")
    if abs(distance) >= count:
        return jnp.zeros_like(block)
    return passed_along(block, "sec", distance)


def exclusive_inflow(rate, drive, sign):
    count = lax.axis_size("sec")

    def fetch(a, b, distance):
        got = received(jnp.concatenate([a, b], axis=0), sign * distance)
        return (got[:1], got[1:])

    near_a, near_b = fetch(rate, drive, 1)
    span = 1
    if count > 2:
        far_a, far_b = fetch(rate, drive, 2)
        near_a, near_b = (near_a * far_a, near_a * far_b + near_b)
        span = 2
    while span < count - 1:
        got_a, got_b = fetch(near_a, near_b, span)
        near_a, near_b = (near_a * got_a, near_a * got_b + near_b)
        span *= 2
    return near_b


def with_halo(array, width):
    parts = [received(array, d) for d in range(width, 0, -1)]
    parts.append(array)
    parts.extend((received(array, -d) for d in range(1, width + 1)))
    return jnp.concatenate(parts, axis=1)


def body(distribution, collision, lower_blocks, upper_blocks, diag_inverse):
    node_count = distribution.shape[0]
    cell_count = distribution.shape[1]
    length = cell_count // TUBES
    node_rows = node_count // NXI
    half_nodes = NXI // 2
    along_x, node_weight, weighted_np, rebuild_np = node_tables(NXI)
    all_mass = jnp.asarray(node_weight, jnp.float32)
    offset = lax.axis_index("vel") * node_count
    weighted = lax.dynamic_slice_in_dim(
        jnp.asarray(weighted_np, jnp.float32), offset, node_count, 1
    )
    rebuild = lax.dynamic_slice_in_dim(jnp.asarray(rebuild_np, jnp.float32), offset, node_count, 1)
    node_mass = lax.dynamic_slice_in_dim(all_mass, offset, node_count, 0)
    line_signed = jnp.asarray(along_x[:NXI], jnp.float32)
    old_moments = lax.psum(jnp.dot(weighted, distribution, precision=HIGH), "vel")
    target = jnp.dot(rebuild.T, old_moments, precision=HIGH)
    total_length = length * lax.axis_size("sec")
    thickness = collision.reshape(1, 1, length, TUBES)
    node_speed = jnp.abs(line_signed).reshape(1, NXI, 1, 1)
    denominator = node_speed * total_length + thickness + pseudo_rate
    carry_rate = node_speed * total_length / denominator
    drive_term = (
        thickness * target.reshape(node_rows, NXI, length, TUBES)
        + pseudo_rate * distribution.reshape(node_rows, NXI, length, TUBES)
    ) / denominator
    prod_neg, local_neg = lax.associative_scan(
        affine_combine,
        (
            jnp.broadcast_to(carry_rate[:, :half_nodes], (1, half_nodes, length, TUBES)),
            drive_term[:, :half_nodes],
        ),
        reverse=True,
        axis=2,
    )
    prod_pos, local_pos = lax.associative_scan(
        affine_combine,
        (
            jnp.broadcast_to(carry_rate[:, half_nodes:], (1, NXI - half_nodes, length, TUBES)),
            drive_term[:, half_nodes:],
        ),
        axis=2,
    )
    inflow_pos = exclusive_inflow(prod_pos[:, :, -1], local_pos[:, :, -1], 1)
    inflow_neg = exclusive_inflow(prod_neg[:, :, 0], local_neg[:, :, 0], -1)
    field_neg = local_neg + prod_neg * inflow_neg[:, :, None, :]
    field_pos = local_pos + prod_pos * inflow_pos[:, :, None, :]
    half_field = jnp.concatenate([field_neg, field_pos], axis=1).reshape(node_count, cell_count)
    half_moments = lax.psum(jnp.dot(weighted, half_field, precision=HIGH), "vel")
    residual = (half_moments - old_moments).reshape(5, length, TUBES)
    width = min(-(-JACOBI // length), lax.axis_size("sec") - 1)
    blocks = jnp.concatenate([lower_blocks, upper_blocks, diag_inverse], axis=0)
    blocks_wide = with_halo(blocks.reshape(75, length, TUBES), width)
    lower_r = blocks_wide[:25]
    upper_r = blocks_wide[25:50]
    inverse_r = blocks_wide[50:]
    residual_wide = with_halo(residual, width)
    correction = apply_block(inverse_r, residual_wide)
    edge_zero = jnp.zeros((5, 1, TUBES), jnp.float32)
    for sweep_index in range(JACOBI):
        from_left = jnp.concatenate([edge_zero, correction[:, :-1]], axis=1)
        from_right = jnp.concatenate([correction[:, 1:], edge_zero], axis=1)
        correction = apply_block(
            inverse_r,
            residual_wide - apply_block(lower_r, from_left) - apply_block(upper_r, from_right),
        )
    correction = correction[:, width * length : (width + 1) * length].reshape(5, cell_count)
    macro = half_moments + correction
    synthetic = half_field + jnp.dot(rebuild.T, correction, precision=HIGH)
    local_totals = jnp.sum(old_moments - macro, axis=1)[0:2]
    magnitude = jnp.sum(jnp.abs(synthetic), axis=1)
    line_loaded = jnp.sum((node_mass * magnitude).reshape(node_rows, NXI), axis=0)
    first_copy = (lax.axis_index("vel") == 0).astype(jnp.float32)
    gathered = lax.psum(jnp.concatenate([line_loaded, local_totals * first_copy]), ("sec", "vel"))
    loaded = gathered[:NXI]
    goals = gathered[NXI:]
    shift_mass = jnp.zeros((), jnp.float32)
    shift_flow = jnp.zeros((), jnp.float32)
    for newton_turn in range(NEWTON):
        sums = newton_sums(loaded, line_signed, shift_mass, shift_flow)
        shift_mass, shift_flow = newton_update(shift_mass, shift_flow, sums, goals[0], goals[1])
    growth = jnp.exp(shift_mass + shift_flow * line_signed)
    synthetic_rows = synthetic.reshape(node_rows, NXI, cell_count)
    new_distribution = synthetic_rows + jnp.abs(synthetic_rows) * (growth[None, :, None] - 1.0)
    return (new_distribution.reshape(node_count, cell_count), macro)


def solution(mesh):
    in_specs = (P("vel", "sec"), P("sec"), P(None, "sec"), P(None, "sec"), P(None, "sec"))
    out_specs = (P("vel", "sec"), P(None, "sec"))
    return jax.shard_map(body, mesh=mesh, in_specs=in_specs, out_specs=out_specs, check_vma=False)
```

profile of v0, /device:TPU:1, one launch (start us, length us, event | category | flops | bytes accessed | tf_op | source)
XLA Modules:
  0.0 254.2 jit_solution(769121284347335400)
XLA Ops:
  1.5 1.7 reshape.255
  4.5 27.9 %psum.21 = f32[5,256]{1,0:T(8,128)S(1)} all-reduce(f32[5,256]{1,0:T(8,128)S(1)} %fusion.13), channel_id=1, replica_groups=mesh['sec'=16,'vel'=16] {'vel'}, use_global_device_ids=true, to_apply=%region_0.0 | all-reduce | flops 1280 | bytes 10240 | tf_op jit(solution)/shard_map/psum | solution.py:172
  32.4 1.8 fusion.16
  36.0 1.3 collective-permute-start
  37.4 1.3 collective-permute-start.1
  38.8 6.2 %collective-permute-start.10 = (f32[75,2,128]{2,1,0:T(2,128)S(1)}, f32[75,2,128]{2,1,0:T(2,128)S(1)}, u32[]{:S(2)}, u32[]{:S(2)}) collective-permute-start(f32[75,2,128]{2,1,0:T(2,128)S(1)} %reshape.257), channel_id=1, source_target_pairs={{0,32},{16,48},{32,64},{48,80},{64,96},{80,112},{96,128},{112,144}... | collective-permute-start | bytes 230408 | tf_op jit(solution)/shard_map/ppermute | solution.py:19
  45.0 3.2 %collective-permute-start.11 = (f32[75,2,128]{2,1,0:T(2,128)S(1)}, f32[75,2,128]{2,1,0:T(2,128)S(1)}, u32[]{:S(2)}, u32[]{:S(2)}) collective-permute-start(f32[75,2,128]{2,1,0:T(2,128)S(1)} %reshape.257), channel_id=1, source_target_pairs={{0,16},{16,32},{32,48},{48,64},{64,80},{80,96},{96,112},{112,128},... | collective-permute-start | bytes 230408 | tf_op jit(solution)/shard_map/ppermute | solution.py:19
  48.3 1.3 collective-permute-start.12
  52.9 4.7 %collective-permute-start.5 = (f32[37,12,128]{2,0,1:T(8,128)S(1)}, f32[37,12,128]{2,0,1:T(8,128)S(1)}, u32[]{:S(2)}, u32[]{:S(2)}) collective-permute-start(f32[37,12,128]{2,0,1:T(8,128)S(1)} %pad_maximum_fusion.5), channel_id=1, source_target_pairs={{0,16},{16,32},{32,48},{48,64},{64,80},{80,96},{96,112},{112,128},... | collective-permute-start | bytes 681992 | tf_op jit(solution)/shard_map/ppermute | solution.py:19
  57.6 6.8 %collective-permute-start.6 = (f32[37,12,128]{2,0,1:T(8,128)S(1)}, f32[37,12,128]{2,0,1:T(8,128)S(1)}, u32[]{:S(2)}, u32[]{:S(2)}) collective-permute-start(f32[37,12,128]{2,0,1:T(8,128)S(1)} %pad_maximum_fusion.5), channel_id=1, source_target_pairs={{0,32},{16,48},{32,64},{48,80},{64,96},{80,112},{96,128},{112,144}... | collective-permute-start | bytes 681992 | tf_op jit(solution)/shard_map/ppermute | solution.py:19
  64.4 2.1 concatenate.91
  66.7 1.3 collective-permute-start.2
  68.8 5.4 %collective-permute-start.7 = (f32[37,12,128]{2,0,1:T(8,128)S(1)}, f32[37,12,128]{2,0,1:T(8,128)S(1)}, u32[]{:S(2)}, u32[]{:S(2)}) collective-permute-start(f32[37,12,128]{2,0,1:T(8,128)S(1)} %pad_maximum_fusion.6), channel_id=1, source_target_pairs={{0,32},{16,48},{32,64},{48,80},{64,96},{80,112},{96,128},{112,144}... | collective-permute-start | bytes 681992 | tf_op jit(solution)/shard_map/ppermute | solution.py:19
  76.8 4.3 %collective-permute-done.7 = f32[37,12,128]{2,0,1:T(8,128)S(1)} collective-permute-done((f32[37,12,128]{2,0,1:T(8,128)S(1)}, f32[37,12,128]{2,0,1:T(8,128)S(1)}, u32[]{:S(2)}, u32[]{:S(2)}) %collective-permute-start.7) | collective-permute-done | bytes 227360 | tf_op jit(solution)/shard_map/ppermute | solution.py:19
  81.3 8.1 %collective-permute-start.8 = (f32[37,12,128]{2,0,1:T(8,128)S(1)}, f32[37,12,128]{2,0,1:T(8,128)S(1)}, u32[]{:S(2)}, u32[]{:S(2)}) collective-permute-start(f32[37,12,128]{2,0,1:T(8,128)S(1)} %pad_maximum_fusion.7), channel_id=1, source_target_pairs={{0,64},{16,80},{32,96},{48,112},{64,128},{80,144},{96,160},{112,17... | collective-permute-start | bytes 681992 | tf_op jit(solution)/shard_map/ppermute | solution.py:19
  89.4 1.5 collective-permute-done.3
  92.6 5.9 %collective-permute-start.9 = (f32[37,12,128]{2,0,1:T(8,128)S(1)}, f32[37,12,128]{2,0,1:T(8,128)S(1)}, u32[]{:S(2)}, u32[]{:S(2)}) collective-permute-start(f32[37,12,128]{2,0,1:T(8,128)S(1)} %pad_maximum_fusion.8), channel_id=1, source_target_pairs={{0,128},{16,144},{32,160},{48,176},{64,192},{80,208},{96,224},{112... | collective-permute-start | bytes 681992 | tf_op jit(solution)/shard_map/ppermute | solution.py:19
  99.5 2.8 %collective-permute-done.9 = f32[37,12,128]{2,0,1:T(8,128)S(1)} collective-permute-done((f32[37,12,128]{2,0,1:T(8,128)S(1)}, f32[37,12,128]{2,0,1:T(8,128)S(1)}, u32[]{:S(2)}, u32[]{:S(2)}) %collective-permute-start.9) | collective-permute-done | bytes 227360 | tf_op jit(solution)/shard_map/ppermute | solution.py:19
  104.8 36.0 %psum.22 = f32[5,256]{1,0:T(8,128)S(1)} all-reduce(f32[5,256]{1,0:T(8,128)S(1)} %fusion), channel_id=1, replica_groups=mesh['sec'=16,'vel'=16] {'vel'}, use_global_device_ids=true, to_apply=%region_1.0 | all-reduce | flops 1280 | bytes 10240 | tf_op jit(solution)/shard_map/psum | solution.py:205
  140.8 2.7 %collective-permute-start.14 = (f32[5,2,128]{2,1,0:T(2,128)S(1)}, f32[5,2,128]{2,1,0:T(2,128)S(1)}, u32[]{:S(2)}, u32[]{:S(2)}) collective-permute-start(f32[5,2,128]{2,1,0:T(2,128)S(1)} %reshape.259), channel_id=1, source_target_pairs={{0,32},{16,48},{32,64},{48,80},{64,96},{80,112},{96,128},{112,144}... | collective-permute-start | bytes 15368 | tf_op jit(solution)/shard_map/ppermute | solution.py:19
  147.5 1.7 collective-permute-done.16
  149.2 2.9 %collective-permute-done.17 = f32[5,2,128]{2,1,0:T(2,128)S(1)} collective-permute-done((f32[5,2,128]{2,1,0:T(2,128)S(1)}, f32[5,2,128]{2,1,0:T(2,128)S(1)}, u32[]{:S(2)}, u32[]{:S(2)}) %collective-permute-start.17) | collective-permute-done | bytes 5152 | tf_op jit(solution)/shard_map/ppermute | solution.py:19
  152.8 1.9 abs_reduce_fusion
  156.4 79.3 %psum.23 = f32[26]{0:T(128)S(1)} all-reduce(f32[26]{0:T(128)S(1)} %pad_maximum_fusion.10), channel_id=1, replica_groups=mesh['sec'=16,'vel'=16] {'sec','vel'}, use_global_device_ids=true, to_apply=%region_18.0 | all-reduce | flops 26 | bytes 208 | tf_op jit(solution)/shard_map/psum | solution.py:230
  (140 shorter events, 25.1 us)
Async XLA Ops:
  0.6 0.7 copy-start.4
  0.6 0.7 copy-start.6
  1.5 1.7 copy-start
  36.0 2.7 %copy-start.1 = (f32[25,256]{1,0:T(8,128)S(1)}, f32[25,256]{1,0:T(8,128)}, u32[]{:S(2)}) copy-start(f32[25,256]{1,0:T(8,128)} %param.13) | copy-start | bytes 76804
  36.0 2.7 %copy-start.2 = (f32[25,256]{1,0:T(8,128)S(1)}, f32[25,256]{1,0:T(8,128)}, u32[]{:S(2)}) copy-start(f32[25,256]{1,0:T(8,128)} %param.12) | copy-start | bytes 76804
  36.0 2.7 %copy-start.3 = (f32[25,256]{1,0:T(8,128)S(1)}, f32[25,256]{1,0:T(8,128)}, u32[]{:S(2)}) copy-start(f32[25,256]{1,0:T(8,128)} %param.11) | copy-start | bytes 76804
  36.0 30.5 %collective-permute-start = (f32[37,12,128]{2,0,1:T(8,128)S(1)}, f32[37,12,128]{2,0,1:T(8,128)S(1)}, u32[]{:S(2)}, u32[]{:S(2)}) collective-permute-start(f32[37,12,128]{2,0,1:T(8,128)S(1)} %pad_maximum_fusion.1), channel_id=1, source_target_pairs={{16,0},{32,16},{48,32},{64,48},{80,64},{96,80},{112,96},{128,112},... | collective-permute-start | bytes 681992 | tf_op jit(solution)/shard_map/ppermute | solution.py:19
  37.4 29.2 %collective-permute-start.1 = (f32[37,12,128]{2,0,1:T(8,128)S(1)}, f32[37,12,128]{2,0,1:T(8,128)S(1)}, u32[]{:S(2)}, u32[]{:S(2)}) collective-permute-start(f32[37,12,128]{2,0,1:T(8,128)S(1)} %pad_maximum_fusion.1), channel_id=1, source_target_pairs={{32,0},{48,16},{64,32},{80,48},{96,64},{112,80},{128,96},{144,112}... | collective-permute-start | bytes 681992 | tf_op jit(solution)/shard_map/ppermute | solution.py:19
  38.8 12.8 %collective-permute-start.10 = (f32[75,2,128]{2,1,0:T(2,128)S(1)}, f32[75,2,128]{2,1,0:T(2,128)S(1)}, u32[]{:S(2)}, u32[]{:S(2)}) collective-permute-start(f32[75,2,128]{2,1,0:T(2,128)S(1)} %reshape.257), channel_id=1, source_target_pairs={{0,32},{16,48},{32,64},{48,80},{64,96},{80,112},{96,128},{112,144}... | collective-permute-start | bytes 230408 | tf_op jit(solution)/shard_map/ppermute | solution.py:19
  45.0 7.9 %collective-permute-start.11 = (f32[75,2,128]{2,1,0:T(2,128)S(1)}, f32[75,2,128]{2,1,0:T(2,128)S(1)}, u32[]{:S(2)}, u32[]{:S(2)}) collective-permute-start(f32[75,2,128]{2,1,0:T(2,128)S(1)} %reshape.257), channel_id=1, source_target_pairs={{0,16},{16,32},{32,48},{48,64},{64,80},{80,96},{96,112},{112,128},... | collective-permute-start | bytes 230408 | tf_op jit(solution)/shard_map/ppermute | solution.py:19
  48.3 9.4 %collective-permute-start.12 = (f32[75,2,128]{2,1,0:T(2,128)S(1)}, f32[75,2,128]{2,1,0:T(2,128)S(1)}, u32[]{:S(2)}, u32[]{:S(2)}) collective-permute-start(f32[75,2,128]{2,1,0:T(2,128)S(1)} %reshape.257), channel_id=1, source_target_pairs={{16,0},{32,16},{48,32},{64,48},{80,64},{96,80},{112,96},{128,112},... | collective-permute-start | bytes 230408 | tf_op jit(solution)/shard_map/ppermute | solution.py:19
  51.6 12.9 %collective-permute-start.13 = (f32[75,2,128]{2,1,0:T(2,128)S(1)}, f32[75,2,128]{2,1,0:T(2,128)S(1)}, u32[]{:S(2)}, u32[]{:S(2)}) collective-permute-start(f32[75,2,128]{2,1,0:T(2,128)S(1)} %reshape.257), channel_id=1, source_target_pairs={{32,0},{48,16},{64,32},{80,48},{96,64},{112,80},{128,96},{144,112}... | collective-permute-start | bytes 230408 | tf_op jit(solution)/shard_map/ppermute | solution.py:19
  52.9 15.1 %collective-permute-start.5 = (f32[37,12,128]{2,0,1:T(8,128)S(1)}, f32[37,12,128]{2,0,1:T(8,128)S(1)}, u32[]{:S(2)}, u32[]{:S(2)}) collective-permute-start(f32[37,12,128]{2,0,1:T(8,128)S(1)} %pad_maximum_fusion.5), channel_id=1, source_target_pairs={{0,16},{16,32},{32,48},{48,64},{64,80},{80,96},{96,112},{112,128},... | collective-permute-start | bytes 681992 | tf_op jit(solution)/shard_map/ppermute | solution.py:19
  57.6 11.1 %collective-permute-start.6 = (f32[37,12,128]{2,0,1:T(8,128)S(1)}, f32[37,12,128]{2,0,1:T(8,128)S(1)}, u32[]{:S(2)}, u32[]{:S(2)}) collective-permute-start(f32[37,12,128]{2,0,1:T(8,128)S(1)} %pad_maximum_fusion.5), channel_id=1, source_target_pairs={{0,32},{16,48},{32,64},{48,80},{64,96},{80,112},{96,128},{112,144}... | collective-permute-start | bytes 681992 | tf_op jit(solution)/shard_map/ppermute | solution.py:19
  66.7 8.7 %collective-permute-start.2 = (f32[37,12,128]{2,0,1:T(8,128)S(1)}, f32[37,12,128]{2,0,1:T(8,128)S(1)}, u32[]{:S(2)}, u32[]{:S(2)}) collective-permute-start(f32[37,12,128]{2,0,1:T(8,128)S(1)} %pad_maximum_fusion.2), channel_id=1, source_target_pairs={{32,0},{48,16},{64,32},{80,48},{96,64},{112,80},{128,96},{144,112}... | collective-permute-start | bytes 681992 | tf_op jit(solution)/shard_map/ppermute | solution.py:19
  68.8 12.3 %collective-permute-start.7 = (f32[37,12,128]{2,0,1:T(8,128)S(1)}, f32[37,12,128]{2,0,1:T(8,128)S(1)}, u32[]{:S(2)}, u32[]{:S(2)}) collective-permute-start(f32[37,12,128]{2,0,1:T(8,128)S(1)} %pad_maximum_fusion.6), channel_id=1, source_target_pairs={{0,32},{16,48},{32,64},{48,80},{64,96},{80,112},{96,128},{112,144}... | collective-permute-start | bytes 681992 | tf_op jit(solution)/shard_map/ppermute | solution.py:19
  75.5 15.4 %collective-permute-start.3 = (f32[37,12,128]{2,0,1:T(8,128)S(1)}, f32[37,12,128]{2,0,1:T(8,128)S(1)}, u32[]{:S(2)}, u32[]{:S(2)}) collective-permute-start(f32[37,12,128]{2,0,1:T(8,128)S(1)} %pad_maximum_fusion.3), channel_id=1, source_target_pairs={{64,0},{80,16},{96,32},{112,48},{128,64},{144,80},{160,96},{176,11... | collective-permute-start | bytes 681992 | tf_op jit(solution)/shard_map/ppermute | solution.py:19
  81.3 11.2 %collective-permute-start.8 = (f32[37,12,128]{2,0,1:T(8,128)S(1)}, f32[37,12,128]{2,0,1:T(8,128)S(1)}, u32[]{:S(2)}, u32[]{:S(2)}) collective-permute-start(f32[37,12,128]{2,0,1:T(8,128)S(1)} %pad_maximum_fusion.7), channel_id=1, source_target_pairs={{0,64},{16,80},{32,96},{48,112},{64,128},{80,144},{96,160},{112,17... | collective-permute-start | bytes 681992 | tf_op jit(solution)/shard_map/ppermute | solution.py:19
  91.0 8.4 %collective-permute-start.4 = (f32[37,12,128]{2,0,1:T(8,128)S(1)}, f32[37,12,128]{2,0,1:T(8,128)S(1)}, u32[]{:S(2)}, u32[]{:S(2)}) collective-permute-start(f32[37,12,128]{2,0,1:T(8,128)S(1)} %pad_maximum_fusion.4), channel_id=1, source_target_pairs={{128,0},{144,16},{160,32},{176,48},{192,64},{208,80},{224,96},{240... | collective-permute-start | bytes 681992 | tf_op jit(solution)/shard_map/ppermute | solution.py:19
  92.6 9.7 %collective-permute-start.9 = (f32[37,12,128]{2,0,1:T(8,128)S(1)}, f32[37,12,128]{2,0,1:T(8,128)S(1)}, u32[]{:S(2)}, u32[]{:S(2)}) collective-permute-start(f32[37,12,128]{2,0,1:T(8,128)S(1)} %pad_maximum_fusion.8), channel_id=1, source_target_pairs={{0,128},{16,144},{32,160},{48,176},{64,192},{80,208},{96,224},{112... | collective-permute-start | bytes 681992 | tf_op jit(solution)/shard_map/ppermute | solution.py:19
  140.8 6.7 %collective-permute-start.14 = (f32[5,2,128]{2,1,0:T(2,128)S(1)}, f32[5,2,128]{2,1,0:T(2,128)S(1)}, u32[]{:S(2)}, u32[]{:S(2)}) collective-permute-start(f32[5,2,128]{2,1,0:T(2,128)S(1)} %reshape.259), channel_id=1, source_target_pairs={{0,32},{16,48},{32,64},{48,80},{64,96},{80,112},{96,128},{112,144}... | collective-permute-start | bytes 15368 | tf_op jit(solution)/shard_map/ppermute | solution.py:19
  143.6 4.0 %collective-permute-start.15 = (f32[5,2,128]{2,1,0:T(2,128)S(1)}, f32[5,2,128]{2,1,0:T(2,128)S(1)}, u32[]{:S(2)}, u32[]{:S(2)}) collective-permute-start(f32[5,2,128]{2,1,0:T(2,128)S(1)} %reshape.259), channel_id=1, source_target_pairs={{0,16},{16,32},{32,48},{48,64},{64,80},{80,96},{96,112},{112,128},... | collective-permute-start | bytes 15368 | tf_op jit(solution)/shard_map/ppermute | solution.py:19
  144.9 4.4 %collective-permute-start.16 = (f32[5,2,128]{2,1,0:T(2,128)S(1)}, f32[5,2,128]{2,1,0:T(2,128)S(1)}, u32[]{:S(2)}, u32[]{:S(2)}) collective-permute-start(f32[5,2,128]{2,1,0:T(2,128)S(1)} %reshape.259), channel_id=1, source_target_pairs={{16,0},{32,16},{48,32},{64,48},{80,64},{96,80},{112,96},{128,112},... | collective-permute-start | bytes 15368 | tf_op jit(solution)/shard_map/ppermute | solution.py:19
  146.2 6.0 %collective-permute-start.17 = (f32[5,2,128]{2,1,0:T(2,128)S(1)}, f32[5,2,128]{2,1,0:T(2,128)S(1)}, u32[]{:S(2)}, u32[]{:S(2)}) collective-permute-start(f32[5,2,128]{2,1,0:T(2,128)S(1)} %reshape.259), channel_id=1, source_target_pairs={{32,0},{48,16},{64,32},{80,48},{96,64},{112,80},{128,96},{144,112}... | collective-permute-start | bytes 15368 | tf_op jit(solution)/shard_map/ppermute | solution.py:19
  (2 other events, 1.3 us)
where the time goes:
time: 255 us; the launch traced here: 254 us
  blocking collectives  143 us (56%)
  starting transfers between devices  56.1 us (22%)
  between operations  16.8 us (7%)
  waiting for transfers between devices  16.2 us (6%)
  other arithmetic  8.25 us (3%)
  local copies, waits for them, and re-layouts  7.31 us (3%)
  matrix products  6.31 us (2%)
    psum x1, blocking collectives, body(): lax.psum(jnp.concatenate([line_loaded, local_totals * first_copy]), ('sec...  79.3 us
    ppermute x18, starting transfers between devices, passed_along(): return lax.ppermute(block, axis, route)  56.1 us
    psum x1, blocking collectives, body(): lax.psum(jnp.dot(weighted, half_field, precision=HIGH), 'vel')  36 us
    psum x1, blocking collectives, body(): lax.psum(jnp.dot(weighted, distribution, precision=HIGH), 'vel')  27.9 us
    ppermute x18, waiting for transfers between devices, passed_along(): return lax.ppermute(block, axis, route)  16.2 us
  transfers between devices with their start and end apart: 18, of which 9 were waited for; matrix products, arithmetic and copies ran while one was open for 2% of the time, Pallas kernels for 0%

commit v1 on v0

--- a/solution.py
+++ b/solution.py
@@ -227,7 +227,8 @@
     magnitude = jnp.sum(jnp.abs(synthetic), axis=1)
     line_loaded = jnp.sum((node_mass * magnitude).reshape(node_rows, NXI), axis=0)
     first_copy = (lax.axis_index("vel") == 0).astype(jnp.float32)
-    gathered = lax.psum(jnp.concatenate([line_loaded, local_totals * first_copy]), ("sec", "vel"))
+    one_axis = lax.psum(jnp.concatenate([line_loaded, local_totals * first_copy]), "vel")
+    gathered = lax.psum(one_axis, "sec")
     loaded = gathered[:NXI]
     goals = gathered[NXI:]
     shift_mass = jnp.zeros((), jnp.float32)

time: 255 us -> 238 us (0.933)
  the two profiles are of different devices: /device:TPU:1 before, /device:TPU:4 now
where the time goes in v1:
time: 238 us; the launch traced here: 237 us
  blocking collectives  108 us (45%)
  starting transfers between devices  67 us (28%)
  waiting for transfers between devices  22.6 us (9%)
  between operations  16.8 us (7%)
  other arithmetic  8.25 us (3%)
  local copies, waits for them, and re-layouts  7.31 us (3%)
  matrix products  6.31 us (3%)
    ppermute x18, starting transfers between devices, passed_along(): return lax.ppermute(block, axis, route)  67 us
    psum x1, blocking collectives, body(): gathered = lax.psum(one_axis, 'sec')  31.5 us
    psum x1, blocking collectives, body(): lax.psum(jnp.dot(weighted, distribution, precision=HIGH), 'vel')  29.3 us
    psum x1, blocking collectives, body(): lax.psum(jnp.dot(weighted, half_field, precision=HIGH), 'vel')  24.1 us
    psum x1, blocking collectives, body(): lax.psum(jnp.concatenate([line_loaded, local_totals * first_copy]), 'vel')  23.5 us
    ppermute x18, waiting for transfers between devices, passed_along(): return lax.ppermute(block, axis, route)  22.6 us
  transfers between devices with their start and end apart: 18, of which 5 were waited for; matrix products, arithmetic and copies ran while one was open for 2% of the time, Pallas kernels for 0%

profile of v1, /device:TPU:4, one launch (start us, length us, event | category | flops | bytes accessed | tf_op | source)
XLA Modules:
  0.0 236.7 jit_solution(7614940818521832031)
XLA Ops:
  4.5 29.3 %psum.28 = f32[5,256]{1,0:T(8,128)S(1)} all-reduce(f32[5,256]{1,0:T(8,128)S(1)} %fusion.13), channel_id=1, replica_groups=mesh['sec'=16,'vel'=16] {'vel'}, use_global_device_ids=true, to_apply=%region_0.0 | all-reduce | flops 1280 | bytes 10240 | tf_op jit(solution)/shard_map/psum | solution.py:172
  37.5 4.9 %collective-permute-start = (f32[37,12,128]{2,0,1:T(8,128)S(1)}, f32[37,12,128]{2,0,1:T(8,128)S(1)}, u32[]{:S(2)}, u32[]{:S(2)}) collective-permute-start(f32[37,12,128]{2,0,1:T(8,128)S(1)} %pad_maximum_fusion.1), channel_id=1, source_target_pairs={{16,0},{32,16},{48,32},{64,48},{80,64},{96,80},{112,96},{128,112},... | collective-permute-start | bytes 681992 | tf_op jit(solution)/shard_map/ppermute | solution.py:19
  42.4 2.5 %collective-permute-start.1 = (f32[37,12,128]{2,0,1:T(8,128)S(1)}, f32[37,12,128]{2,0,1:T(8,128)S(1)}, u32[]{:S(2)}, u32[]{:S(2)}) collective-permute-start(f32[37,12,128]{2,0,1:T(8,128)S(1)} %pad_maximum_fusion.1), channel_id=1, source_target_pairs={{32,0},{48,16},{64,32},{80,48},{96,64},{112,80},{128,96},{144,112}... | collective-permute-start | bytes 681992 | tf_op jit(solution)/shard_map/ppermute | solution.py:19
  45.0 4.8 %collective-permute-start.10 = (f32[75,2,128]{2,1,0:T(2,128)S(1)}, f32[75,2,128]{2,1,0:T(2,128)S(1)}, u32[]{:S(2)}, u32[]{:S(2)}) collective-permute-start(f32[75,2,128]{2,1,0:T(2,128)S(1)} %reshape.257), channel_id=1, source_target_pairs={{0,32},{16,48},{32,64},{48,80},{64,96},{80,112},{96,128},{112,144}... | collective-permute-start | bytes 230408 | tf_op jit(solution)/shard_map/ppermute | solution.py:19
  51.8 6.0 %collective-permute-start.12 = (f32[75,2,128]{2,1,0:T(2,128)S(1)}, f32[75,2,128]{2,1,0:T(2,128)S(1)}, u32[]{:S(2)}, u32[]{:S(2)}) collective-permute-start(f32[75,2,128]{2,1,0:T(2,128)S(1)} %reshape.257), channel_id=1, source_target_pairs={{16,0},{32,16},{48,32},{64,48},{80,64},{96,80},{112,96},{128,112},... | collective-permute-start | bytes 230408 | tf_op jit(solution)/shard_map/ppermute | solution.py:19
  61.8 2.8 %collective-permute-start.5 = (f32[37,12,128]{2,0,1:T(8,128)S(1)}, f32[37,12,128]{2,0,1:T(8,128)S(1)}, u32[]{:S(2)}, u32[]{:S(2)}) collective-permute-start(f32[37,12,128]{2,0,1:T(8,128)S(1)} %pad_maximum_fusion.5), channel_id=1, source_target_pairs={{0,16},{16,32},{32,48},{48,64},{64,80},{80,96},{96,112},{112,128},... | collective-permute-start | bytes 681992 | tf_op jit(solution)/shard_map/ppermute | solution.py:19
  64.6 4.6 %collective-permute-start.6 = (f32[37,12,128]{2,0,1:T(8,128)S(1)}, f32[37,12,128]{2,0,1:T(8,128)S(1)}, u32[]{:S(2)}, u32[]{:S(2)}) collective-permute-start(f32[37,12,128]{2,0,1:T(8,128)S(1)} %pad_maximum_fusion.5), channel_id=1, source_target_pairs={{0,32},{16,48},{32,64},{48,80},{64,96},{80,112},{96,128},{112,144}... | collective-permute-start | bytes 681992 | tf_op jit(solution)/shard_map/ppermute | solution.py:19
  69.2 2.1 concatenate.91
  71.4 3.7 %collective-permute-start.2 = (f32[37,12,128]{2,0,1:T(8,128)S(1)}, f32[37,12,128]{2,0,1:T(8,128)S(1)}, u32[]{:S(2)}, u32[]{:S(2)}) collective-permute-start(f32[37,12,128]{2,0,1:T(8,128)S(1)} %pad_maximum_fusion.2), channel_id=1, source_target_pairs={{32,0},{48,16},{64,32},{80,48},{96,64},{112,80},{128,96},{144,112}... | collective-permute-start | bytes 681992 | tf_op jit(solution)/shard_map/ppermute | solution.py:19
  76.3 11.3 %collective-permute-start.7 = (f32[37,12,128]{2,0,1:T(8,128)S(1)}, f32[37,12,128]{2,0,1:T(8,128)S(1)}, u32[]{:S(2)}, u32[]{:S(2)}) collective-permute-start(f32[37,12,128]{2,0,1:T(8,128)S(1)} %pad_maximum_fusion.6), channel_id=1, source_target_pairs={{0,32},{16,48},{32,64},{48,80},{64,96},{80,112},{96,128},{112,144}... | collective-permute-start | bytes 681992 | tf_op jit(solution)/shard_map/ppermute | solution.py:19
  87.7 2.4 %collective-permute-start.3 = (f32[37,12,128]{2,0,1:T(8,128)S(1)}, f32[37,12,128]{2,0,1:T(8,128)S(1)}, u32[]{:S(2)}, u32[]{:S(2)}) collective-permute-start(f32[37,12,128]{2,0,1:T(8,128)S(1)} %pad_maximum_fusion.3), channel_id=1, source_target_pairs={{64,0},{80,16},{96,32},{112,48},{128,64},{144,80},{160,96},{176,11... | collective-permute-start | bytes 681992 | tf_op jit(solution)/shard_map/ppermute | solution.py:19
  90.2 4.2 %collective-permute-done.7 = f32[37,12,128]{2,0,1:T(8,128)S(1)} collective-permute-done((f32[37,12,128]{2,0,1:T(8,128)S(1)}, f32[37,12,128]{2,0,1:T(8,128)S(1)}, u32[]{:S(2)}, u32[]{:S(2)}) %collective-permute-start.7) | collective-permute-done | bytes 227360 | tf_op jit(solution)/shard_map/ppermute | solution.py:19
  94.4 3.4 %collective-permute-start.8 = (f32[37,12,128]{2,0,1:T(8,128)S(1)}, f32[37,12,128]{2,0,1:T(8,128)S(1)}, u32[]{:S(2)}, u32[]{:S(2)}) collective-permute-start(f32[37,12,128]{2,0,1:T(8,128)S(1)} %pad_maximum_fusion.7), channel_id=1, source_target_pairs={{0,64},{16,80},{32,96},{48,112},{64,128},{80,144},{96,160},{112,17... | collective-permute-start | bytes 681992 | tf_op jit(solution)/shard_map/ppermute | solution.py:19
  99.3 5.4 %collective-permute-done.8 = f32[37,12,128]{2,0,1:T(8,128)S(1)} collective-permute-done((f32[37,12,128]{2,0,1:T(8,128)S(1)}, f32[37,12,128]{2,0,1:T(8,128)S(1)}, u32[]{:S(2)}, u32[]{:S(2)}) %collective-permute-start.8) | collective-permute-done | bytes 227360 | tf_op jit(solution)/shard_map/ppermute | solution.py:19
  106.2 8.2 %collective-permute-done.9 = f32[37,12,128]{2,0,1:T(8,128)S(1)} collective-permute-done((f32[37,12,128]{2,0,1:T(8,128)S(1)}, f32[37,12,128]{2,0,1:T(8,128)S(1)}, u32[]{:S(2)}, u32[]{:S(2)}) %collective-permute-start.9) | collective-permute-done | bytes 227360 | tf_op jit(solution)/shard_map/ppermute | solution.py:19
  116.9 24.1 %psum.29 = f32[5,256]{1,0:T(8,128)S(1)} all-reduce(f32[5,256]{1,0:T(8,128)S(1)} %fusion), channel_id=1, replica_groups=mesh['sec'=16,'vel'=16] {'vel'}, use_global_device_ids=true, to_apply=%region_1.0 | all-reduce | flops 1280 | bytes 10240 | tf_op jit(solution)/shard_map/psum | solution.py:205
  141.0 3.0 %collective-permute-start.14 = (f32[5,2,128]{2,1,0:T(2,128)S(1)}, f32[5,2,128]{2,1,0:T(2,128)S(1)}, u32[]{:S(2)}, u32[]{:S(2)}) collective-permute-start(f32[5,2,128]{2,1,0:T(2,128)S(1)} %reshape.259), channel_id=1, source_target_pairs={{0,32},{16,48},{32,64},{48,80},{64,96},{80,112},{96,128},{112,144}... | collective-permute-start | bytes 15368 | tf_op jit(solution)/shard_map/ppermute | solution.py:19
  144.0 1.9 collective-permute-start.15
  145.9 6.0 %collective-permute-start.16 = (f32[5,2,128]{2,1,0:T(2,128)S(1)}, f32[5,2,128]{2,1,0:T(2,128)S(1)}, u32[]{:S(2)}, u32[]{:S(2)}) collective-permute-start(f32[5,2,128]{2,1,0:T(2,128)S(1)} %reshape.259), channel_id=1, source_target_pairs={{16,0},{32,16},{48,32},{64,48},{80,64},{96,80},{112,96},{128,112},... | collective-permute-start | bytes 15368 | tf_op jit(solution)/shard_map/ppermute | solution.py:19
  152.0 3.1 %collective-permute-start.17 = (f32[5,2,128]{2,1,0:T(2,128)S(1)}, f32[5,2,128]{2,1,0:T(2,128)S(1)}, u32[]{:S(2)}, u32[]{:S(2)}) collective-permute-start(f32[5,2,128]{2,1,0:T(2,128)S(1)} %reshape.259), channel_id=1, source_target_pairs={{32,0},{48,16},{64,32},{80,48},{96,64},{112,80},{128,96},{144,112}... | collective-permute-start | bytes 15368 | tf_op jit(solution)/shard_map/ppermute | solution.py:19
  155.2 3.8 %collective-permute-done.17 = f32[5,2,128]{2,1,0:T(2,128)S(1)} collective-permute-done((f32[5,2,128]{2,1,0:T(2,128)S(1)}, f32[5,2,128]{2,1,0:T(2,128)S(1)}, u32[]{:S(2)}, u32[]{:S(2)}) %collective-permute-start.17) | collective-permute-done | bytes 5152 | tf_op jit(solution)/shard_map/ppermute | solution.py:19
  159.7 1.9 abs_reduce_fusion
  163.3 23.5 %psum.30 = f32[26]{0:T(128)S(1)} all-reduce(f32[26]{0:T(128)S(1)} %pad_maximum_fusion.10), channel_id=1, replica_groups=mesh['sec'=16,'vel'=16] {'vel'}, use_global_device_ids=true, to_apply=%region_18.0 | all-reduce | flops 26 | bytes 208 | tf_op jit(solution)/shard_map/psum | solution.py:230
  186.8 31.5 %psum.31 = f32[26]{0:T(128)S(1)} all-reduce(f32[26]{0:T(128)S(1)} %psum.30), channel_id=1, replica_groups=mesh['sec'=16,'vel'=16] {'sec'}, use_global_device_ids=true, to_apply=%region_19.0 | all-reduce | flops 26 | bytes 208 | tf_op jit(solution)/shard_map/psum | solution.py:231
  (141 shorter events, 25.4 us)
Async XLA Ops:
  0.6 0.7 copy-start.4
  0.6 0.7 copy-start.6
  1.5 1.7 copy-start
  37.4 7.5 %copy-start.1 = (f32[25,256]{1,0:T(8,128)S(1)}, f32[25,256]{1,0:T(8,128)}, u32[]{:S(2)}) copy-start(f32[25,256]{1,0:T(8,128)} %param.13) | copy-start | bytes 76804
  37.4 7.5 %copy-start.2 = (f32[25,256]{1,0:T(8,128)S(1)}, f32[25,256]{1,0:T(8,128)}, u32[]{:S(2)}) copy-start(f32[25,256]{1,0:T(8,128)} %param.12) | copy-start | bytes 76804
  37.4 7.5 %copy-start.3 = (f32[25,256]{1,0:T(8,128)S(1)}, f32[25,256]{1,0:T(8,128)}, u32[]{:S(2)}) copy-start(f32[25,256]{1,0:T(8,128)} %param.11) | copy-start | bytes 76804
  37.5 33.8 %collective-permute-start = (f32[37,12,128]{2,0,1:T(8,128)S(1)}, f32[37,12,128]{2,0,1:T(8,128)S(1)}, u32[]{:S(2)}, u32[]{:S(2)}) collective-permute-start(f32[37,12,128]{2,0,1:T(8,128)S(1)} %pad_maximum_fusion.1), channel_id=1, source_target_pairs={{16,0},{32,16},{48,32},{64,48},{80,64},{96,80},{112,96},{128,112},... | collective-permute-start | bytes 681992 | tf_op jit(solution)/shard_map/ppermute | solution.py:19
  42.4 28.9 %collective-permute-start.1 = (f32[37,12,128]{2,0,1:T(8,128)S(1)}, f32[37,12,128]{2,0,1:T(8,128)S(1)}, u32[]{:S(2)}, u32[]{:S(2)}) collective-permute-start(f32[37,12,128]{2,0,1:T(8,128)S(1)} %pad_maximum_fusion.1), channel_id=1, source_target_pairs={{32,0},{48,16},{64,32},{80,48},{96,64},{112,80},{128,96},{144,112}... | collective-permute-start | bytes 681992 | tf_op jit(solution)/shard_map/ppermute | solution.py:19
  45.0 14.8 %collective-permute-start.10 = (f32[75,2,128]{2,1,0:T(2,128)S(1)}, f32[75,2,128]{2,1,0:T(2,128)S(1)}, u32[]{:S(2)}, u32[]{:S(2)}) collective-permute-start(f32[75,2,128]{2,1,0:T(2,128)S(1)} %reshape.257), channel_id=1, source_target_pairs={{0,32},{16,48},{32,64},{48,80},{64,96},{80,112},{96,128},{112,144}... | collective-permute-start | bytes 230408 | tf_op jit(solution)/shard_map/ppermute | solution.py:19
  49.9 11.9 %collective-permute-start.11 = (f32[75,2,128]{2,1,0:T(2,128)S(1)}, f32[75,2,128]{2,1,0:T(2,128)S(1)}, u32[]{:S(2)}, u32[]{:S(2)}) collective-permute-start(f32[75,2,128]{2,1,0:T(2,128)S(1)} %reshape.257), channel_id=1, source_target_pairs={{0,16},{16,32},{32,48},{48,64},{64,80},{80,96},{96,112},{112,128},... | collective-permute-start | bytes 230408 | tf_op jit(solution)/shard_map/ppermute | solution.py:19
  51.8 12.8 %collective-permute-start.12 = (f32[75,2,128]{2,1,0:T(2,128)S(1)}, f32[75,2,128]{2,1,0:T(2,128)S(1)}, u32[]{:S(2)}, u32[]{:S(2)}) collective-permute-start(f32[75,2,128]{2,1,0:T(2,128)S(1)} %reshape.257), channel_id=1, source_target_pairs={{16,0},{32,16},{48,32},{64,48},{80,64},{96,80},{112,96},{128,112},... | collective-permute-start | bytes 230408 | tf_op jit(solution)/shard_map/ppermute | solution.py:19
  59.8 9.3 %collective-permute-start.13 = (f32[75,2,128]{2,1,0:T(2,128)S(1)}, f32[75,2,128]{2,1,0:T(2,128)S(1)}, u32[]{:S(2)}, u32[]{:S(2)}) collective-permute-start(f32[75,2,128]{2,1,0:T(2,128)S(1)} %reshape.257), channel_id=1, source_target_pairs={{32,0},{48,16},{64,32},{80,48},{96,64},{112,80},{128,96},{144,112}... | collective-permute-start | bytes 230408 | tf_op jit(solution)/shard_map/ppermute | solution.py:19
  61.8 13.3 %collective-permute-start.5 = (f32[37,12,128]{2,0,1:T(8,128)S(1)}, f32[37,12,128]{2,0,1:T(8,128)S(1)}, u32[]{:S(2)}, u32[]{:S(2)}) collective-permute-start(f32[37,12,128]{2,0,1:T(8,128)S(1)} %pad_maximum_fusion.5), channel_id=1, source_target_pairs={{0,16},{16,32},{32,48},{48,64},{64,80},{80,96},{96,112},{112,128},... | collective-permute-start | bytes 681992 | tf_op jit(solution)/shard_map/ppermute | solution.py:19
  64.6 11.6 %collective-permute-start.6 = (f32[37,12,128]{2,0,1:T(8,128)S(1)}, f32[37,12,128]{2,0,1:T(8,128)S(1)}, u32[]{:S(2)}, u32[]{:S(2)}) collective-permute-start(f32[37,12,128]{2,0,1:T(8,128)S(1)} %pad_maximum_fusion.5), channel_id=1, source_target_pairs={{0,32},{16,48},{32,64},{48,80},{64,96},{80,112},{96,128},{112,144}... | collective-permute-start | bytes 681992 | tf_op jit(solution)/shard_map/ppermute | solution.py:19
  71.4 16.2 %collective-permute-start.2 = (f32[37,12,128]{2,0,1:T(8,128)S(1)}, f32[37,12,128]{2,0,1:T(8,128)S(1)}, u32[]{:S(2)}, u32[]{:S(2)}) collective-permute-start(f32[37,12,128]{2,0,1:T(8,128)S(1)} %pad_maximum_fusion.2), channel_id=1, source_target_pairs={{32,0},{48,16},{64,32},{80,48},{96,64},{112,80},{128,96},{144,112}... | collective-permute-start | bytes 681992 | tf_op jit(solution)/shard_map/ppermute | solution.py:19
  76.3 18.0 %collective-permute-start.7 = (f32[37,12,128]{2,0,1:T(8,128)S(1)}, f32[37,12,128]{2,0,1:T(8,128)S(1)}, u32[]{:S(2)}, u32[]{:S(2)}) collective-permute-start(f32[37,12,128]{2,0,1:T(8,128)S(1)} %pad_maximum_fusion.6), channel_id=1, source_target_pairs={{0,32},{16,48},{32,64},{48,80},{64,96},{80,112},{96,128},{112,144}... | collective-permute-start | bytes 681992 | tf_op jit(solution)/shard_map/ppermute | solution.py:19
  87.7 10.2 %collective-permute-start.3 = (f32[37,12,128]{2,0,1:T(8,128)S(1)}, f32[37,12,128]{2,0,1:T(8,128)S(1)}, u32[]{:S(2)}, u32[]{:S(2)}) collective-permute-start(f32[37,12,128]{2,0,1:T(8,128)S(1)} %pad_maximum_fusion.3), channel_id=1, source_target_pairs={{64,0},{80,16},{96,32},{112,48},{128,64},{144,80},{160,96},{176,11... | collective-permute-start | bytes 681992 | tf_op jit(solution)/shard_map/ppermute | solution.py:19
  94.4 10.2 %collective-permute-start.8 = (f32[37,12,128]{2,0,1:T(8,128)S(1)}, f32[37,12,128]{2,0,1:T(8,128)S(1)}, u32[]{:S(2)}, u32[]{:S(2)}) collective-permute-start(f32[37,12,128]{2,0,1:T(8,128)S(1)} %pad_maximum_fusion.7), channel_id=1, source_target_pairs={{0,64},{16,80},{32,96},{48,112},{64,128},{80,144},{96,160},{112,17... | collective-permute-start | bytes 681992 | tf_op jit(solution)/shard_map/ppermute | solution.py:19
  98.0 8.1 %collective-permute-start.4 = (f32[37,12,128]{2,0,1:T(8,128)S(1)}, f32[37,12,128]{2,0,1:T(8,128)S(1)}, u32[]{:S(2)}, u32[]{:S(2)}) collective-permute-start(f32[37,12,128]{2,0,1:T(8,128)S(1)} %pad_maximum_fusion.4), channel_id=1, source_target_pairs={{128,0},{144,16},{160,32},{176,48},{192,64},{208,80},{224,96},{240... | collective-permute-start | bytes 681992 | tf_op jit(solution)/shard_map/ppermute | solution.py:19
  104.8 9.6 %collective-permute-start.9 = (f32[37,12,128]{2,0,1:T(8,128)S(1)}, f32[37,12,128]{2,0,1:T(8,128)S(1)}, u32[]{:S(2)}, u32[]{:S(2)}) collective-permute-start(f32[37,12,128]{2,0,1:T(8,128)S(1)} %pad_maximum_fusion.8), channel_id=1, source_target_pairs={{0,128},{16,144},{32,160},{48,176},{64,192},{80,208},{96,224},{112... | collective-permute-start | bytes 681992 | tf_op jit(solution)/shard_map/ppermute | solution.py:19
  141.0 14.2 %collective-permute-start.14 = (f32[5,2,128]{2,1,0:T(2,128)S(1)}, f32[5,2,128]{2,1,0:T(2,128)S(1)}, u32[]{:S(2)}, u32[]{:S(2)}) collective-permute-start(f32[5,2,128]{2,1,0:T(2,128)S(1)} %reshape.259), channel_id=1, source_target_pairs={{0,32},{16,48},{32,64},{48,80},{64,96},{80,112},{96,128},{112,144}... | collective-permute-start | bytes 15368 | tf_op jit(solution)/shard_map/ppermute | solution.py:19
  144.0 11.1 %collective-permute-start.15 = (f32[5,2,128]{2,1,0:T(2,128)S(1)}, f32[5,2,128]{2,1,0:T(2,128)S(1)}, u32[]{:S(2)}, u32[]{:S(2)}) collective-permute-start(f32[5,2,128]{2,1,0:T(2,128)S(1)} %reshape.259), channel_id=1, source_target_pairs={{0,16},{16,32},{32,48},{48,64},{64,80},{80,96},{96,112},{112,128},... | collective-permute-start | bytes 15368 | tf_op jit(solution)/shard_map/ppermute | solution.py:19
  145.9 9.2 %collective-permute-start.16 = (f32[5,2,128]{2,1,0:T(2,128)S(1)}, f32[5,2,128]{2,1,0:T(2,128)S(1)}, u32[]{:S(2)}, u32[]{:S(2)}) collective-permute-start(f32[5,2,128]{2,1,0:T(2,128)S(1)} %reshape.259), channel_id=1, source_target_pairs={{16,0},{32,16},{48,32},{64,48},{80,64},{96,80},{112,96},{128,112},... | collective-permute-start | bytes 15368 | tf_op jit(solution)/shard_map/ppermute | solution.py:19
  152.0 7.0 %collective-permute-start.17 = (f32[5,2,128]{2,1,0:T(2,128)S(1)}, f32[5,2,128]{2,1,0:T(2,128)S(1)}, u32[]{:S(2)}, u32[]{:S(2)}) collective-permute-start(f32[5,2,128]{2,1,0:T(2,128)S(1)} %reshape.259), channel_id=1, source_target_pairs={{32,0},{48,16},{64,32},{80,48},{96,64},{112,80},{128,96},{144,112}... | collective-permute-start | bytes 15368 | tf_op jit(solution)/shard_map/ppermute | solution.py:19
  (2 other events, 1.3 us)
